TPU v7x, 512 devices: a whole 4x4x16 slice. The times are simulated.
512 devices in a mesh: wide: 64 (over x, z), narrow: 8 (over y, core).
Axes of the slice: x: 4, y: 4, z: 16, core: 2. Of those that a mesh axis runs over, the one named last changes fastest.
Arguments:
- tokens: bfloat16 [49152, 2048], P('wide', 'narrow'), may hold values from -6 to 6
- norm_gain: float32 [2048], replicated, may hold values from 0.1 to 1.9
- qkv_weight: bfloat16 [2048, 3, 2048], P('wide', None, 'narrow'), may hold values from -0.125 to 0.125
- out_weight: bfloat16 [2048, 2048], P('wide', 'narrow'), may hold values from -0.25 to 0.25
- cache_pool: bfloat16 [1536, 128, 2, 2048], P('wide', None, None, 'narrow'), may hold values from -400 to 400, as said below
- prefix_pool: bfloat16 [2048, 2, 2048], P('wide', None, 'narrow'), may hold values from -6 to 6
- page_table: int32 [64, 24], P('wide'), may hold values from 0 to 23, each once within a row
- cache_len: int32 [64], P('wide'), may hold values from 512 to 3072
- group_ids: int32 [64], P('wide'), may hold values from 0 to 7, as said below
- group_pages: int32 [16], replicated, may hold values from 0 to 15, each once
Outputs:
- branch_out: bfloat16 [49152, 2048], P('wide', 'narrow')
- new_pages: bfloat16 [49152, 2, 2048], P('wide', None, 'narrow')
Inputs may be any that keep to these rules, and one draw needn't show every extreme that they name: `page_table`: each row is a permutation of the 24 pages of that request. `group_ids`: each group has 8 requests. `group_pages`: a permutation of the prefix pool's pages. `cache_pool`: keys are stored already rotated.
All inputs are finite; a program needn't handle non-finite values.
Results may differ from a plain program's by a relative error of at most 0.0095.
The roundings to bfloat16 on the way count: a program that leaves them out, or rounds other values in their place, can miss the bound.
Values may be sent and summed in bfloat16 or wider, within the bound.
No kernel may reach another device: no remote copies, remote signals or barrier semaphores. Data moves between devices by JAX's collectives and lax.ppermute only.
A program may use at most 128 MiB of HBM per device.

v0:
```python
import jax
import jax.numpy as jnp
from jax import lax
from jax.sharding import Mesh, PartitionSpec as P

HEAD_DIM = 64
ROT = 16
PAGE = 128
KB = 8
PPAGES = 2
NEGATIVE = -1e30


def rotary(vectors, positions):
    half_rot = ROT // 2
    frequency = 10000.0 ** (-(jnp.arange(half_rot, dtype=jnp.float32) * 2.0 / ROT))
    angles = positions.astype(jnp.float32)[:, None] * frequency[None, :]
    cos_part = jnp.concatenate([jnp.cos(angles), jnp.cos(angles)], axis=1)[:, None, :]
    sine_part = jnp.concatenate([jnp.sin(angles), jnp.sin(angles)], axis=1)[:, None, :]
    rotated_in = vectors[..., :ROT]
    turned = jnp.concatenate([-rotated_in[..., half_rot:], rotated_in[..., :half_rot]], axis=-1)
    return jnp.concatenate(
        [rotated_in * cos_part + turned * sine_part, vectors[..., ROT:]], axis=-1
    )


def attend(running, queries, keys, values, key_valid):
    row_max, weight_sum, weighted = running
    scores = jnp.einsum("qhd,khd->hqk", queries, keys, preferred_element_type=jnp.float32) * 0.125
    scores = jnp.where(key_valid[None], scores, NEGATIVE)
    new_max = jnp.maximum(row_max, jnp.max(scores, axis=2))
    expo = jnp.where(key_valid[None], jnp.exp(scores - new_max[:, :, None]), 0.0)
    factor = jnp.exp(row_max - new_max)
    weight_sum = weight_sum * factor + jnp.sum(expo, axis=2)
    update = jnp.einsum(
        "hqk,khd->qhd", expo.astype(jnp.bfloat16), values, preferred_element_type=jnp.float32
    )
    weighted = weighted * jnp.transpose(factor)[:, :, None] + update
    return (new_max, weight_sum, weighted)


def gather_columns(part):
    count = lax.axis_size("narrow")
    copies = jnp.broadcast_to(part[None], (count,) + part.shape)
    received = lax.all_to_all(copies, "narrow", 0, 0, tiled=False)
    return jnp.transpose(received, (1, 0, 2)).reshape(part.shape[0], count * part.shape[1])


def local(
    tokens,
    norm_gain,
    qkv_weight,
    out_weight,
    cache_pool,
    prefix_pool,
    page_table,
    cache_len,
    group_ids,
    group_pages,
):
    span_rows = tokens.shape[0]
    local_width = qkv_weight.shape[2]
    heads_here = local_width // HEAD_DIM
    gathered = gather_columns(tokens)
    widened = gathered.astype(jnp.float32)
    row_mean = jnp.mean(widened, axis=1, keepdims=True)
    centered = widened - row_mean
    variance = jnp.mean(centered * centered, axis=1, keepdims=True)
    normed = (centered * lax.rsqrt(variance + 1e-05) * norm_gain).astype(jnp.bfloat16)
    shard_rows = qkv_weight.shape[0]
    merged = jnp.concatenate(
        [
            qkv_weight.reshape(shard_rows, 3 * local_width),
            out_weight,
            prefix_pool.reshape(shard_rows, 2 * local_width),
        ],
        axis=1,
    )
    along_x = lax.axis_size("wx")
    by_x = lax.all_to_all(
        jnp.broadcast_to(merged[None], (along_x,) + merged.shape), "wx", 0, 0, tiled=False
    )
    by_xz = lax.all_gather(by_x, "wz", axis=0, tiled=False)
    merged_whole = jnp.transpose(by_xz, (1, 0, 2, 3)).reshape(-1, merged.shape[1])
    piece_rows = merged_whole[:, : 3 * local_width]
    out_rows = merged_whole[:, 3 * local_width : 4 * local_width]
    prefix_whole = merged_whole[:, 4 * local_width :]
    piece_count = piece_rows.shape[0]
    columns = normed
    projected = jnp.dot(
        columns,
        piece_rows.reshape(piece_count, 3 * local_width),
        preferred_element_type=jnp.float32,
    )
    projected = projected.reshape(span_rows, 3, heads_here, HEAD_DIM)
    length = cache_len[0]
    offset = jnp.arange(span_rows, dtype=jnp.int32)
    positions = PPAGES * PAGE + length + offset
    queries = rotary(projected[:, 0], positions).astype(jnp.bfloat16)
    keys = rotary(projected[:, 1], positions).astype(jnp.bfloat16)
    values = projected[:, 2].astype(jnp.bfloat16)
    new_pages = jnp.stack(
        [keys.reshape(span_rows, local_width), values.reshape(span_rows, local_width)], axis=1
    )
    initial = (
        jnp.full((heads_here, span_rows), NEGATIVE, jnp.float32),
        jnp.zeros((heads_here, span_rows), jnp.float32),
        jnp.zeros((span_rows, heads_here, HEAD_DIM), jnp.float32),
    )
    running = attend(initial, queries, keys, values, offset[:, None] >= offset[None, :])
    my_group = group_ids[0]
    chosen = lax.dynamic_slice_in_dim(group_pages, my_group * PPAGES, PPAGES)
    key_rows = jnp.concatenate(
        [
            lax.dynamic_slice_in_dim(prefix_whole, chosen[k] * PAGE, PAGE, axis=0)
            for k in range(PPAGES)
        ],
        axis=0,
    ).reshape(PPAGES * PAGE, 2, heads_here, HEAD_DIM)
    running = attend(
        running,
        queries,
        key_rows[:, 0],
        key_rows[:, 1],
        jnp.ones((span_rows, PPAGES * PAGE), dtype=bool),
    )
    page_list = page_table[0]
    page_count = cache_pool.shape[0]
    slot_of_page = (
        jnp.zeros((page_count,), jnp.int32)
        .at[page_list]
        .set(jnp.arange(page_count, dtype=jnp.int32))
    )
    block_keys = KB * PAGE
    key_offset = jnp.arange(block_keys, dtype=jnp.int32)

    def cache_block(block_index, state_now):
        key_rows = lax.dynamic_slice_in_dim(cache_pool, block_index * KB, KB, axis=0).reshape(
            block_keys, 2, heads_here, HEAD_DIM
        )
        slots = lax.dynamic_slice_in_dim(slot_of_page, block_index * KB, KB)
        key_slot = jnp.repeat(slots, PAGE) * PAGE + key_offset % PAGE
        key_valid = jnp.broadcast_to((key_slot < length)[None, :], (span_rows, block_keys))
        return attend(state_now, queries, key_rows[:, 0], key_rows[:, 1], key_valid)

    running = lax.fori_loop(0, page_count // KB, cache_block, running)
    head_values = (
        (running[2] / jnp.transpose(running[1])[:, :, None])
        .astype(jnp.bfloat16)
        .reshape(span_rows, local_width)
    )
    all_heads = lax.all_gather(head_values, "narrow", axis=1, tiled=True)
    columns = all_heads
    branch_out = jnp.dot(columns, out_rows, preferred_element_type=jnp.float32)
    return (branch_out.astype(jnp.bfloat16), new_pages)


def split_mesh(mesh):
    grid = mesh.devices
    try:
        along_x = len({device.coords[0] for device in grid[:, 0]})
    except (AttributeError, TypeError):
        along_x = 4
    shape = (along_x, grid.shape[0] // along_x, grid.shape[1])
    return Mesh(grid.reshape(shape), ("wx", "wz", "narrow"))


def solution(mesh):
    W = ("wx", "wz")
    placed = (
        P(W, "narrow"),
        P(),
        P(W, None, "narrow"),
        P(W, "narrow"),
        P(W, None, None, "narrow"),
        P(W, None, "narrow"),
        P(W, None),
        P(W),
        P(W),
        P(),
    )
    return jax.shard_map(
        local,
        mesh=split_mesh(mesh),
        in_specs=placed,
        out_specs=(P(W, "narrow"), P(W, None, "narrow")),
        check_vma=False,
    )
```

profile of v0, /device:TPU:1, one launch (start us, length us, event | category | flops | bytes accessed | tf_op | source)
XLA Modules:
  0.0 230.6 jit_solution(7096636370363122591)
XLA Ops:
  9.6 11.0 %all_to_all.10 = bf16[4,32,1536]{2,1,0:T(8,128)(2,1)} all-to-all(bf16[4,32,1536]{2,1,0:T(8,128)(2,1)S(1)} %broadcast_in_dim.158), channel_id=1, replica_groups=mesh['wx'=4,'wz'=16,'narrow'=8] {'wx'}, dimensions={0} | all-to-all | bytes 786432 | tf_op jit(solution)/shard_map/all_to_all | solution.py:80
  20.6 2.8 %broadcast_in_dim.157 = bf16[8,768,256]{2,1,0:T(8,128)(2,1)} broadcast(bf16[768,256]{1,0:T(8,128)(2,1)} %param.12), dimensions={1,2} | broadcast | bytes 3538944 | tf_op jit(solution)/shard_map/broadcast_in_dim | solution.py:44
  23.4 10.7 %all-to-all-start = ((bf16[8,768,256]{2,1,0:T(8,128)(2,1)}), bf16[8,768,256]{2,1,0:T(8,128)(2,1)}, u32[]{:S(2)}, u32[]{:S(2)}) async-start(bf16[8,768,256]{2,1,0:T(8,128)(2,1)} %broadcast_in_dim.157), calls=%async_computation | async-start | bytes 6291456 | tf_op jit(solution)/shard_map/all_to_all | solution.py:45
  39.9 31.7 %all-to-all-done = bf16[8,768,256]{2,1,0:T(8,128)(2,1)} async-done(((bf16[8,768,256]{2,1,0:T(8,128)(2,1)}), bf16[8,768,256]{2,1,0:T(8,128)(2,1)}, u32[]{:S(2)}, u32[]{:S(2)}) %all-to-all-start) | async-done | bytes 3145760 | tf_op jit(solution)/shard_map/all_to_all | solution.py:45
  71.6 3.2 %copy.39 = bf16[8,768,256]{1,2,0:T(8,128)(2,1)S(1)} copy(bf16[8,768,256]{2,1,0:T(8,128)(2,1)} %all-to-all-done) | data formatting | bytes 6291456 | tf_op jit(solution)/shard_map/all_to_all | solution.py:45
  76.2 2.6 %fusion.35 = bf16[8,768,256]{1,2,0:T(8,128)(2,1)} fusion(bf16[8,768,256]{1,2,0:T(8,128)(2,1)S(1)} %copy.39, f32[8,256]{1,0:T(8,128)S(1)} %mul.207, f32[768]{0:T(1024)S(1)} %add_rsqrt_fusion, f32[768]{0:T(1024)S(1)} %broadcast_multiply_fusion), kind=kLoop, calls=%fused_computation.44 | loop fusion | flops 7864320 | bytes 6305792 | tf_op jit(solution)/shard_map/convert.3
  78.9 29.6 %all-gather.6.cloned.1.call-done = bf16[64,32,1536]{2,1,0:T(8,128)(2,1)} async-done(((bf16[4,32,1536]{2,1,0:T(8,128)(2,1)}), bf16[64,32,1536]{2,1,0:T(8,128)(2,1)}) %all-gather.6.cloned.1.call-update) | async-done | bytes 6291472 | tf_op jit(solution)/shard_map/all_gather | solution.py:83
  108.5 3.5 %copy.41 = bf16[4,16,32,1536]{3,2,1,0:T(8,128)(2,1)S(1)} copy(bf16[4,16,32,1536]{3,2,0,1:T(8,128)(2,1)} %bitcast.126) | data formatting | bytes 12582912 | tf_op jit(solution)/shard_map/transpose | solution.py:84
  112.0 1.6 slice.114
  113.6 1.6 copy-done
  115.5 3.0 %copy.42 = bf16[768,2048]{1,0:T(8,128)(2,1)} copy(bf16[768,2048]{0,1:T(8,128)(2,1)S(1)} %slice_bitcast_fusion.4) | data formatting | bytes 6291456 | tf_op jit(solution)/shard_map/dot_general | solution.py:90
  118.4 5.6 %fusion.80 = f32[768,3,4,64]{0,3,2,1:T(8,128)S(1)} fusion(bf16[768,2048,1,1]{0,1,3,2:T(8,128)(2,1)} %bitcast.127, bf16[3,4,64,2048]{3,2,1,0:T(8,128)(2,1)} %bitcast.128), kind=kOutput, calls=%fused_computation.115 | convolution fusion | flops 2415919104 | bytes 8650752 | tf_op jit(solution)/shard_map/dot_general | solution.py:90
  130.1 1.8 fusion.28
  132.0 2.3 %fusion.32 = f32[4,768]{1,0:T(4,128)S(1)} fusion(f32[4,768,768]{1,2,0:T(8,128)S(1)} %get-tuple-element.355, f32[4,768]{1,0:T(4,128)S(1)} %get-tuple-element.348, pred[768,768]{0,1:T(8,128)(4,1)S(1)} %copy-done.1), kind=kLoop, calls=%fused_computation.41 | loop fusion | flops 11793408 | bytes 10051584 | tf_op jit(solution)/shard_map/reduce_sum | solution.py:34
  134.3 3.9 %fusion.57 = f32[768,4,64]{0,2,1:T(8,128)S(1)} fusion(f32[4,768,768]{1,2,0:T(8,128)S(1)} %get-tuple-element.355, f32[4,768]{1,0:T(4,128)S(1)} %get-tuple-element.348, pred[768,768]{0,1:T(8,128)(4,1)S(1)} %copy-done.1, f32[768,4]{0,1:T(4,128)S(1)} %get-tuple-element.347, f32[768,4]{0,1:T(4,128)S(1)} %get-tuple-element.346, f32[768,3,4,64]{0,3,2,1:T(8,128)} %copy-done.2), kind=kOutput, calls=%fused_computation.60 | convolution fusion | flops 314179584 | bytes 11243520 | tf_op jit(solution)/shard_map/hqk,khd->qhd/dot_general | solution.py:35
  139.5 43.8 %while.21 = (s32[]{:T(128)}, f32[4,768]{1,0:T(4,128)S(1)}, f32[4,768]{1,0:T(4,128)S(1)}, f32[768,4,64]{0,2,1:T(8,128)S(1)}, s32[24]{0:T(128)S(1)}, /*index=5*/s3...) while((s32[]{:T(128)}, f32[4,768]{1,0:T(4,128)S(1)}, ...), condition=%wide.region_10.11_spmd.clone, body=%wide.region_7.10_spmd.clone.sunk | while | flops 846611456 | bytes 47256848 | solution.py:146
  140.6 1.9 constant_dynamic-slice_fusion.4
  142.5 1.5 copy.59
  144.5 2.7 %bitcast_reduce_fusion.2 = (f32[4,768]{1,0:T(4,128)S(1)}, f32[4,1024,768]{2,1,0:T(8,128)S(1)}) fusion(pred[1024]{0:T(1024)(128)(4,1)S(1)} %fusion.93, bf16[768,4,64]{0,2,1:T(8,128)(2,1)S(1)} %get-tuple-element.450, bf16[1024,2,4,64]{0,3,2,1:T(8,128)(2,1)S(1)} %reshape.194), kind=kOutput, calls=%fused_computation.4.clone.1 | convolution fusion | flops 412087296 | bytes 13513728 | tf_op jit(solution)/shard_map/while/body/eval_jaxpr/qhd,khd->hqk/dot_general | solution.py:29
  147.2 3.0 %fusion.96 = f32[768,4,64]{0,2,1:T(8,128)S(1)} fusion(f32[4,1024,768]{2,1,0:T(8,128)S(1)} %get-tuple-element.417, f32[4,768]{1,0:T(4,128)S(1)} %get-tuple-element.444, pred[1024]{0:T(1024)(128)(4,1)S(1)} %fusion.93, f32[768,4,64]{0,2,1:T(8,128)S(1)} %get-tuple-element.434, bf16[1024,2,4,64]{0,3,2,1:T(8,128)(2,1)S(1)} %reshape.194, ...), kind=kOutput, calls=%fused_computation.14.clone.1 | convolution fusion | flops 418775040 | bytes 14706688 | tf_op jit(solution)/shard_map/while/body/eval_jaxpr/hqk,khd->qhd/dot_general | solution.py:35
  150.2 4.0 %fusion.95 = f32[4,768]{1,0:T(4,128)S(1)} fusion(f32[4,1024,768]{2,1,0:T(8,128)S(1)} %get-tuple-element.417, f32[4,768]{1,0:T(4,128)S(1)} %get-tuple-element.444, pred[1024]{0:T(1024)(128)(4,1)S(1)} %fusion.93), kind=kLoop, calls=%fused_computation.9.clone.1 | loop fusion | flops 15725568 | bytes 12608512 | tf_op jit(solution)/shard_map/while/body/eval_jaxpr/reduce_sum | solution.py:34
  155.1 1.9 constant_dynamic-slice_fusion.4
  159.0 2.7 %bitcast_reduce_fusion.2 = (f32[4,768]{1,0:T(4,128)S(1)}, f32[4,1024,768]{2,1,0:T(8,128)S(1)}) fusion(pred[1024]{0:T(1024)(128)(4,1)S(1)} %fusion.93, bf16[768,4,64]{0,2,1:T(8,128)(2,1)S(1)} %get-tuple-element.450, bf16[1024,2,4,64]{0,3,2,1:T(8,128)(2,1)S(1)} %reshape.194), kind=kOutput, calls=%fused_computation.4.clone.1 | convolution fusion | flops 412087296 | bytes 13513728 | tf_op jit(solution)/shard_map/while/body/eval_jaxpr/qhd,khd->hqk/dot_general | solution.py:29
  161.7 3.0 %fusion.96 = f32[768,4,64]{0,2,1:T(8,128)S(1)} fusion(f32[4,1024,768]{2,1,0:T(8,128)S(1)} %get-tuple-element.417, f32[4,768]{1,0:T(4,128)S(1)} %get-tuple-element.444, pred[1024]{0:T(1024)(128)(4,1)S(1)} %fusion.93, f32[768,4,64]{0,2,1:T(8,128)S(1)} %get-tuple-element.434, bf16[1024,2,4,64]{0,3,2,1:T(8,128)(2,1)S(1)} %reshape.194, ...), kind=kOutput, calls=%fused_computation.14.clone.1 | convolution fusion | flops 418775040 | bytes 14706688 | tf_op jit(solution)/shard_map/while/body/eval_jaxpr/hqk,khd->qhd/dot_general | solution.py:35
  164.7 4.0 %fusion.95 = f32[4,768]{1,0:T(4,128)S(1)} fusion(f32[4,1024,768]{2,1,0:T(8,128)S(1)} %get-tuple-element.417, f32[4,768]{1,0:T(4,128)S(1)} %get-tuple-element.444, pred[1024]{0:T(1024)(128)(4,1)S(1)} %fusion.93), kind=kLoop, calls=%fused_computation.9.clone.1 | loop fusion | flops 15725568 | bytes 12608512 | tf_op jit(solution)/shard_map/while/body/eval_jaxpr/reduce_sum | solution.py:34
  169.6 1.9 constant_dynamic-slice_fusion.4
  173.5 2.7 %bitcast_reduce_fusion.2 = (f32[4,768]{1,0:T(4,128)S(1)}, f32[4,1024,768]{2,1,0:T(8,128)S(1)}) fusion(pred[1024]{0:T(1024)(128)(4,1)S(1)} %fusion.93, bf16[768,4,64]{0,2,1:T(8,128)(2,1)S(1)} %get-tuple-element.450, bf16[1024,2,4,64]{0,3,2,1:T(8,128)(2,1)S(1)} %reshape.194), kind=kOutput, calls=%fused_computation.4.clone.1 | convolution fusion | flops 412087296 | bytes 13513728 | tf_op jit(solution)/shard_map/while/body/eval_jaxpr/qhd,khd->hqk/dot_general | solution.py:29
  176.2 3.0 %fusion.96 = f32[768,4,64]{0,2,1:T(8,128)S(1)} fusion(f32[4,1024,768]{2,1,0:T(8,128)S(1)} %get-tuple-element.417, f32[4,768]{1,0:T(4,128)S(1)} %get-tuple-element.444, pred[1024]{0:T(1024)(128)(4,1)S(1)} %fusion.93, f32[768,4,64]{0,2,1:T(8,128)S(1)} %get-tuple-element.434, bf16[1024,2,4,64]{0,3,2,1:T(8,128)(2,1)S(1)} %reshape.194, ...), kind=kOutput, calls=%fused_computation.14.clone.1 | convolution fusion | flops 418775040 | bytes 14706688 | tf_op jit(solution)/shard_map/while/body/eval_jaxpr/hqk,khd->qhd/dot_general | solution.py:35
  179.3 4.0 %fusion.95 = f32[4,768]{1,0:T(4,128)S(1)} fusion(f32[4,1024,768]{2,1,0:T(8,128)S(1)} %get-tuple-element.417, f32[4,768]{1,0:T(4,128)S(1)} %get-tuple-element.444, pred[1024]{0:T(1024)(128)(4,1)S(1)} %fusion.93), kind=kLoop, calls=%fused_computation.9.clone.1 | loop fusion | flops 15725568 | bytes 12608512 | tf_op jit(solution)/shard_map/while/body/eval_jaxpr/reduce_sum | solution.py:34
  187.6 2.7 %pad_maximum_fusion = bf16[768,2,256]{2,1,0:T(2,128)(2,1)} fusion(bf16[768,1,256]{2,1,0:T(2,128)(2,1)S(1)} %copy.49, bf16[768,1,256]{2,1,0:T(2,128)(2,1)S(1)} %copy.48), kind=kLoop, calls=%fused_computation.67 | loop fusion | flops 1572864 | bytes 1572864 | tf_op jit(solution)/shard_map/stack | solution.py:102
  190.3 29.6 %all-gather.4.cloned.1.call-done = bf16[768,2048]{0,1:T(8,128)(2,1)} async-done(((bf16[768,256]{0,1:T(8,128)(2,1)}), bf16[768,2048]{0,1:T(8,128)(2,1)}) %all-gather.4.cloned.1.call-update) | async-done | bytes 3145744 | tf_op jit(solution)/shard_map/all_gather | solution.py:152
  219.8 3.9 %convolution_convert_fusion = bf16[768,256]{1,0:T(8,128)(2,1)} fusion(bf16[768,2048]{0,1:T(8,128)(2,1)} %all-gather.4.cloned.1.call-done, bf16[2048,1536]{1,0:T(8,128)(2,1)} %bitcast.125), kind=kOutput, calls=%fused_computation.61 | convolution fusion | flops 805502976 | bytes 4587520 | tf_op jit(solution)/shard_map/dot_general | solution.py:154
  (82 shorter events, 25.6 us)
Async XLA Ops:
  7.2 27.6 %copy-start.7 = (s32[16]{0:T(128)S(1)}, s32[16]{0:T(128)}, u32[]{:S(2)}) copy-start(s32[16]{0:T(128)} %param.21) | copy-start | bytes 196
  7.2 30.2 %copy-start.6 = (f32[2048]{0:T(1024)S(1)}, f32[2048]{0:T(1024)}, u32[]{:S(2)}) copy-start(f32[2048]{0:T(1024)} %param.13) | copy-start | bytes 24580
  7.2 30.2 %copy-start.8 = (s32[1,24]{1,0:T(1,128)S(1)}, s32[1,24]{1,0:T(1,128)}, u32[]{:S(2)}) copy-start(s32[1,24]{1,0:T(1,128)} %param.18) | copy-start | bytes 292
  7.2 101.3 %all-gather.6.cloned.1.call-start = ((), (), s32[]{:S(2)}) async-start(), calls=%async_computation.3 | async-start | bytes 6684672 | tf_op jit(solution)/shard_map/all_gather | solution.py:83
  23.4 48.2 %all-to-all-start = ((bf16[8,768,256]{2,1,0:T(8,128)(2,1)}), bf16[8,768,256]{2,1,0:T(8,128)(2,1)}, u32[]{:S(2)}, u32[]{:S(2)}) async-start(bf16[8,768,256]{2,1,0:T(8,128)(2,1)} %broadcast_in_dim.157), calls=%async_computation | async-start | bytes 6291456 | tf_op jit(solution)/shard_map/all_to_all | solution.py:45
  34.1 185.8 %all-gather.4.cloned.1.call-start = ((), (), s32[]{:S(2)}) async-start(), calls=%async_computation.2 | async-start | bytes 3538944 | tf_op jit(solution)/shard_map/all_gather | solution.py:152
  112.0 3.3 %copy-start = (bf16[4,16,32,1536]{3,2,1,0:T(8,128)(2,1)}, bf16[4,16,32,1536]{3,2,1,0:T(8,128)(2,1)S(1)}, u32[]{:S(2)}) copy-start(bf16[4,16,32,1536]{3,2,1,0:T(8,128)(2,1)S(1)} %copy.41) | copy-start | bytes 18874372
  124.0 1.4 copy-start.2
  124.0 6.0 %copy-start.1 = (pred[768,768]{0,1:T(8,128)(4,1)S(1)}, pred[768,768]{0,1:T(8,128)(4,1)}, u32[]{:S(2)}) copy-start(pred[768,768]{0,1:T(8,128)(4,1)} %iota_compare_fusion) | copy-start | bytes 1769476
  125.5 6.4 %copy-start.3 = (bf16[768,4,48]{0,2,1:T(8,128)(2,1)}, bf16[768,4,48]{0,2,1:T(8,128)(2,1)S(1)}, u32[]{:S(2)}) copy-start(bf16[768,4,48]{0,2,1:T(8,128)(2,1)S(1)} %slice.113) | copy-start | bytes 884740
  130.1 4.2 %copy-start.4 = (bf16[768,4,16]{0,2,1:T(8,128)(2,1)}, bf16[768,4,16]{0,2,1:T(8,128)(2,1)S(1)}, u32[]{:S(2)}) copy-start(bf16[768,4,16]{0,2,1:T(8,128)(2,1)S(1)} %fusion.62) | copy-start | bytes 294916
  139.5 46.4 %copy-start.5 = (bf16[768,4,16]{0,2,1:T(8,128)(2,1)S(1)}, bf16[768,4,16]{0,2,1:T(8,128)(2,1)}, u32[]{:S(2)}) copy-start(bf16[768,4,16]{0,2,1:T(8,128)(2,1)} %copy-done.4) | copy-start | bytes 294916
Sparse Core Ops, SparseCore 0:
  20.7 87.7 all-gather.5
  184.3 35.5 all-gather.3
where the time goes:
time: 232 us; the launch traced here: 231 us
  waiting for transfers between devices  90.9 us (39%)
  local copies, waits for them, and re-layouts  35.6 us (15%)
  matrix products  33.6 us (14%)
  other arithmetic  31.3 us (13%)
  between operations  17 us (7%)
  blocking collectives  11 us (5%)
  starting transfers between devices  10.7 us (5%)
    all_to_all x1, waiting for transfers between devices, gather_columns(): received = lax.all_to_all(copies, 'narrow', 0, 0, tiled=False)  31.7 us
    all_gather x1, waiting for transfers between devices, local(): by_xz = lax.all_gather(by_x, 'wz', axis=0, tiled=False)  29.6 us
    all_gather x1, waiting for transfers between devices, local(): all_heads = lax.all_gather(head_values, 'narrow', axis=1, tiled=True)  29.6 us
    reduce_sum x5, other arithmetic, attend(): weight_sum = weight_sum * factor + jnp.sum(expo, axis=2)  14.9 us
    dot_general x5, matrix products, attend(): jnp.einsum('hqk,khd->qhd', expo.astype(jnp.bfloat16), values, preferred_e...  13.7 us
    all_to_all x1, blocking collectives, local(): lax.all_to_all(jnp.broadcast_to(merged[None], (along_x,) + merged.shape),...  11 us
    all_to_all x1, starting transfers between devices, gather_columns(): received = lax.all_to_all(copies, 'narrow', 0, 0, tiled=False)  10.7 us
    dot_general x5, matrix products, attend(): jnp.einsum('qhd,khd->hqk', queries, keys, preferred_element_type=jnp.floa...  10.4 us
  transfers between devices with their start and end apart: 3, of which 3 were waited for; matrix products, arithmetic and copies ran while one was open for 8% of the time, Pallas kernels for 0%

commit v1 on v0

--- a/solution.py
+++ b/solution.py
@@ -149,7 +149,9 @@
         .astype(jnp.bfloat16)
         .reshape(span_rows, local_width)
     )
-    all_heads = lax.all_gather(head_values, "narrow", axis=1, tiled=True)
+    all_heads = jnp.concatenate(
+        lax.all_to_all(jnp.stack([head_values] * lax.axis_size("narrow")), "narrow", 0, 0), axis=1
+    )
     columns = all_heads
     branch_out = jnp.dot(columns, out_rows, preferred_element_type=jnp.float32)
     return (branch_out.astype(jnp.bfloat16), new_pages)

time: 232 us -> 242 us (1.043)
  starting transfers between devices: 10.7 us -> 18.9 us
  local copies, waits for them, and re-layouts: 35.6 us -> 39.8 us
    all_gather x1 -> x0, waiting for transfers between devices: 29.6 us -> none  [local(): all_heads = lax.all_gather(head_values, 'narrow', axis=1, tiled=True)]
    all_to_all x0 -> x1, waiting for transfers between devices: none -> 27.8 us  [local(): lax.all_to_all(jnp.stack([head_values] * lax.axis_size('narrow')), 'narro...]
    all_to_all x0 -> x1, starting transfers between devices: none -> 8.21 us  [local(): lax.all_to_all(jnp.stack([head_values] * lax.axis_size('narrow')), 'narro...]
  transfers between devices with their start and end apart: 3 -> 3, of which waited for: 3 -> 3; matrix products, arithmetic and copies ran while one was open for 8% -> 9% of each run, Pallas kernels for 0% -> 0%
where the time goes in v1:
time: 242 us; the launch traced here: 241 us
  waiting for transfers between devices  89.2 us (37%)
  local copies, waits for them, and re-layouts  39.8 us (16%)
  matrix products  32.7 us (14%)
  other arithmetic  31.8 us (13%)
  starting transfers between devices  18.9 us (8%)
  between operations  17 us (7%)
  blocking collectives  11 us (5%)
    all_to_all x1, waiting for transfers between devices, gather_columns(): received = lax.all_to_all(copies, 'narrow', 0, 0, tiled=False)  31.7 us
    all_gather x1, waiting for transfers between devices, local(): by_xz = lax.all_gather(by_x, 'wz', axis=0, tiled=False)  29.6 us
    all_to_all x1, waiting for transfers between devices, local(): lax.all_to_all(jnp.stack([head_values] * lax.axis_size('narrow')), 'narro...  27.8 us
    reduce_sum x5, other arithmetic, attend(): weight_sum = weight_sum * factor + jnp.sum(expo, axis=2)  14.9 us
    dot_general x5, matrix products, attend(): jnp.einsum('hqk,khd->qhd', expo.astype(jnp.bfloat16), values, preferred_e...  13.7 us
    all_to_all x1, blocking collectives, local(): lax.all_to_all(jnp.broadcast_to(merged[None], (along_x,) + merged.shape),...  11 us
    all_to_all x1, starting transfers between devices, gather_columns(): received = lax.all_to_all(copies, 'narrow', 0, 0, tiled=False)  10.7 us
    dot_general x5, matrix products, attend(): jnp.einsum('qhd,khd->hqk', queries, keys, preferred_element_type=jnp.floa...  10.4 us
  transfers between devices with their start and end apart: 3, of which 3 were waited for; matrix products, arithmetic and copies ran while one was open for 9% of the time, Pallas kernels for 0%

profile of v1, /device:TPU:1, one launch (start us, length us, event | category | flops | bytes accessed | tf_op | source)
XLA Modules:
  0.0 240.8 jit_solution(1803324508484641983)
XLA Ops:
  9.6 11.0 %all_to_all.15 = bf16[4,32,1536]{2,1,0:T(8,128)(2,1)} all-to-all(bf16[4,32,1536]{2,1,0:T(8,128)(2,1)S(1)} %broadcast_in_dim.158), channel_id=1, replica_groups=mesh['wx'=4,'wz'=16,'narrow'=8] {'wx'}, dimensions={0} | all-to-all | bytes 786432 | tf_op jit(solution)/shard_map/all_to_all | solution.py:80
  20.6 2.8 %broadcast_in_dim.157 = bf16[8,768,256]{2,1,0:T(8,128)(2,1)} broadcast(bf16[768,256]{1,0:T(8,128)(2,1)} %param.12), dimensions={1,2} | broadcast | bytes 3538944 | tf_op jit(solution)/shard_map/broadcast_in_dim | solution.py:44
  23.4 10.7 %all-to-all-start = ((bf16[8,768,256]{2,1,0:T(8,128)(2,1)}), bf16[8,768,256]{2,1,0:T(8,128)(2,1)}, u32[]{:S(2)}, u32[]{:S(2)}) async-start(bf16[8,768,256]{2,1,0:T(8,128)(2,1)} %broadcast_in_dim.157), calls=%async_computation | async-start | bytes 6291456 | tf_op jit(solution)/shard_map/all_to_all | solution.py:45
  39.9 31.7 %all-to-all-done = bf16[8,768,256]{2,1,0:T(8,128)(2,1)} async-done(((bf16[8,768,256]{2,1,0:T(8,128)(2,1)}), bf16[8,768,256]{2,1,0:T(8,128)(2,1)}, u32[]{:S(2)}, u32[]{:S(2)}) %all-to-all-start) | async-done | bytes 3145760 | tf_op jit(solution)/shard_map/all_to_all | solution.py:45
  71.6 3.2 %copy.40 = bf16[8,768,256]{1,2,0:T(8,128)(2,1)S(1)} copy(bf16[8,768,256]{2,1,0:T(8,128)(2,1)} %all-to-all-done) | data formatting | bytes 6291456 | tf_op jit(solution)/shard_map/all_to_all | solution.py:45
  76.2 2.6 %fusion.35 = bf16[8,768,256]{1,2,0:T(8,128)(2,1)} fusion(bf16[8,768,256]{1,2,0:T(8,128)(2,1)S(1)} %copy.40, f32[8,256]{1,0:T(8,128)S(1)} %mul.207, f32[768]{0:T(1024)S(1)} %add_rsqrt_fusion, f32[768]{0:T(1024)S(1)} %broadcast_multiply_fusion), kind=kLoop, calls=%fused_computation.44 | loop fusion | flops 7864320 | bytes 6305792 | tf_op jit(solution)/shard_map/convert.3
  78.9 29.6 %all-gather.3.cloned.1.call-done = bf16[64,32,1536]{2,1,0:T(8,128)(2,1)} async-done(((bf16[4,32,1536]{2,1,0:T(8,128)(2,1)}), bf16[64,32,1536]{2,1,0:T(8,128)(2,1)}) %all-gather.3.cloned.1.call-update) | async-done | bytes 6291472 | tf_op jit(solution)/shard_map/all_gather | solution.py:83
  108.5 3.5 %copy.42 = bf16[4,16,32,1536]{3,2,1,0:T(8,128)(2,1)S(1)} copy(bf16[4,16,32,1536]{3,2,0,1:T(8,128)(2,1)} %bitcast.129) | data formatting | bytes 12582912 | tf_op jit(solution)/shard_map/transpose | solution.py:84
  115.5 3.0 %copy.43 = bf16[768,2048]{1,0:T(8,128)(2,1)} copy(bf16[768,2048]{0,1:T(8,128)(2,1)S(1)} %slice_bitcast_fusion.4) | data formatting | bytes 6291456 | tf_op jit(solution)/shard_map/dot_general | solution.py:90
  118.4 5.6 %fusion.80 = f32[768,3,4,64]{0,3,2,1:T(8,128)S(1)} fusion(bf16[768,2048,1,1]{0,1,3,2:T(8,128)(2,1)} %bitcast.131, bf16[3,4,64,2048]{3,2,1,0:T(8,128)(2,1)} %bitcast.132), kind=kOutput, calls=%fused_computation.115 | convolution fusion | flops 2415919104 | bytes 8650752 | tf_op jit(solution)/shard_map/dot_general | solution.py:90
  130.1 1.8 fusion.28
  132.0 2.3 fusion.32
  134.3 3.9 %fusion.57 = f32[768,4,64]{0,2,1:T(8,128)S(1)} fusion(f32[4,768,768]{1,2,0:T(8,128)S(1)} %get-tuple-element.355, f32[4,768]{1,0:T(4,128)S(1)} %get-tuple-element.348, pred[768,768]{0,1:T(8,128)(4,1)S(1)} %copy-done.1, f32[768,4]{0,1:T(4,128)S(1)} %get-tuple-element.347, f32[768,4]{0,1:T(4,128)S(1)} %get-tuple-element.346, f32[768,3,4,64]{0,3,2,1:T(8,128)} %copy-done.2), kind=kOutput, calls=%fused_computation.60 | convolution fusion | flops 314179584 | bytes 11243520 | tf_op jit(solution)/shard_map/hqk,khd->qhd/dot_general | solution.py:35
  139.5 43.8 %while.21 = (s32[]{:T(128)}, f32[4,768]{1,0:T(4,128)S(1)}, f32[4,768]{1,0:T(4,128)S(1)}, f32[768,4,64]{0,2,1:T(8,128)S(1)}, s32[24]{0:T(128)S(1)}, /*index=5*/s3...) while((s32[]{:T(128)}, f32[4,768]{1,0:T(4,128)S(1)}, ...), condition=%wide.region_10.11_spmd.clone, body=%wide.region_7.10_spmd.clone.sunk | while | flops 846611456 | bytes 47256848 | solution.py:146
  140.6 1.9 constant_dynamic-slice_fusion.4
  144.5 2.7 %bitcast_reduce_fusion.2 = (f32[4,768]{1,0:T(4,128)S(1)}, f32[4,1024,768]{2,1,0:T(8,128)S(1)}) fusion(pred[1024]{0:T(1024)(128)(4,1)S(1)} %fusion.93, bf16[768,4,64]{0,2,1:T(8,128)(2,1)S(1)} %get-tuple-element.450, bf16[1024,2,4,64]{0,3,2,1:T(8,128)(2,1)S(1)} %reshape.200), kind=kOutput, calls=%fused_computation.4.clone.1 | convolution fusion | flops 412087296 | bytes 13513728 | tf_op jit(solution)/shard_map/while/body/eval_jaxpr/qhd,khd->hqk/dot_general | solution.py:29
  147.2 3.0 %fusion.96 = f32[768,4,64]{0,2,1:T(8,128)S(1)} fusion(f32[4,1024,768]{2,1,0:T(8,128)S(1)} %get-tuple-element.417, f32[4,768]{1,0:T(4,128)S(1)} %get-tuple-element.444, pred[1024]{0:T(1024)(128)(4,1)S(1)} %fusion.93, f32[768,4,64]{0,2,1:T(8,128)S(1)} %get-tuple-element.434, bf16[1024,2,4,64]{0,3,2,1:T(8,128)(2,1)S(1)} %reshape.200, ...), kind=kOutput, calls=%fused_computation.14.clone.1 | convolution fusion | flops 418775040 | bytes 14706688 | tf_op jit(solution)/shard_map/while/body/eval_jaxpr/hqk,khd->qhd/dot_general | solution.py:35
  150.2 4.0 %fusion.95 = f32[4,768]{1,0:T(4,128)S(1)} fusion(f32[4,1024,768]{2,1,0:T(8,128)S(1)} %get-tuple-element.417, f32[4,768]{1,0:T(4,128)S(1)} %get-tuple-element.444, pred[1024]{0:T(1024)(128)(4,1)S(1)} %fusion.93), kind=kLoop, calls=%fused_computation.9.clone.1 | loop fusion | flops 15725568 | bytes 12608512 | tf_op jit(solution)/shard_map/while/body/eval_jaxpr/reduce_sum | solution.py:34
  155.1 1.9 constant_dynamic-slice_fusion.4
  159.0 2.7 %bitcast_reduce_fusion.2 = (f32[4,768]{1,0:T(4,128)S(1)}, f32[4,1024,768]{2,1,0:T(8,128)S(1)}) fusion(pred[1024]{0:T(1024)(128)(4,1)S(1)} %fusion.93, bf16[768,4,64]{0,2,1:T(8,128)(2,1)S(1)} %get-tuple-element.450, bf16[1024,2,4,64]{0,3,2,1:T(8,128)(2,1)S(1)} %reshape.200), kind=kOutput, calls=%fused_computation.4.clone.1 | convolution fusion | flops 412087296 | bytes 13513728 | tf_op jit(solution)/shard_map/while/body/eval_jaxpr/qhd,khd->hqk/dot_general | solution.py:29
  161.7 3.0 %fusion.96 = f32[768,4,64]{0,2,1:T(8,128)S(1)} fusion(f32[4,1024,768]{2,1,0:T(8,128)S(1)} %get-tuple-element.417, f32[4,768]{1,0:T(4,128)S(1)} %get-tuple-element.444, pred[1024]{0:T(1024)(128)(4,1)S(1)} %fusion.93, f32[768,4,64]{0,2,1:T(8,128)S(1)} %get-tuple-element.434, bf16[1024,2,4,64]{0,3,2,1:T(8,128)(2,1)S(1)} %reshape.200, ...), kind=kOutput, calls=%fused_computation.14.clone.1 | convolution fusion | flops 418775040 | bytes 14706688 | tf_op jit(solution)/shard_map/while/body/eval_jaxpr/hqk,khd->qhd/dot_general | solution.py:35
  164.7 4.0 %fusion.95 = f32[4,768]{1,0:T(4,128)S(1)} fusion(f32[4,1024,768]{2,1,0:T(8,128)S(1)} %get-tuple-element.417, f32[4,768]{1,0:T(4,128)S(1)} %get-tuple-element.444, pred[1024]{0:T(1024)(128)(4,1)S(1)} %fusion.93), kind=kLoop, calls=%fused_computation.9.clone.1 | loop fusion | flops 15725568 | bytes 12608512 | tf_op jit(solution)/shard_map/while/body/eval_jaxpr/reduce_sum | solution.py:34
  169.6 1.9 constant_dynamic-slice_fusion.4
  173.5 2.7 %bitcast_reduce_fusion.2 = (f32[4,768]{1,0:T(4,128)S(1)}, f32[4,1024,768]{2,1,0:T(8,128)S(1)}) fusion(pred[1024]{0:T(1024)(128)(4,1)S(1)} %fusion.93, bf16[768,4,64]{0,2,1:T(8,128)(2,1)S(1)} %get-tuple-element.450, bf16[1024,2,4,64]{0,3,2,1:T(8,128)(2,1)S(1)} %reshape.200), kind=kOutput, calls=%fused_computation.4.clone.1 | convolution fusion | flops 412087296 | bytes 13513728 | tf_op jit(solution)/shard_map/while/body/eval_jaxpr/qhd,khd->hqk/dot_general | solution.py:29
  176.2 3.0 %fusion.96 = f32[768,4,64]{0,2,1:T(8,128)S(1)} fusion(f32[4,1024,768]{2,1,0:T(8,128)S(1)} %get-tuple-element.417, f32[4,768]{1,0:T(4,128)S(1)} %get-tuple-element.444, pred[1024]{0:T(1024)(128)(4,1)S(1)} %fusion.93, f32[768,4,64]{0,2,1:T(8,128)S(1)} %get-tuple-element.434, bf16[1024,2,4,64]{0,3,2,1:T(8,128)(2,1)S(1)} %reshape.200, ...), kind=kOutput, calls=%fused_computation.14.clone.1 | convolution fusion | flops 418775040 | bytes 14706688 | tf_op jit(solution)/shard_map/while/body/eval_jaxpr/hqk,khd->qhd/dot_general | solution.py:35
  179.3 4.0 %fusion.95 = f32[4,768]{1,0:T(4,128)S(1)} fusion(f32[4,1024,768]{2,1,0:T(8,128)S(1)} %get-tuple-element.417, f32[4,768]{1,0:T(4,128)S(1)} %get-tuple-element.444, pred[1024]{0:T(1024)(128)(4,1)S(1)} %fusion.93), kind=kLoop, calls=%fused_computation.9.clone.1 | loop fusion | flops 15725568 | bytes 12608512 | tf_op jit(solution)/shard_map/while/body/eval_jaxpr/reduce_sum | solution.py:34
  183.4 1.9 stack.6
  185.3 8.2 %all-to-all-start.2 = ((bf16[8,768,256]{1,2,0:T(8,128)(2,1)}), bf16[8,768,256]{1,2,0:T(8,128)(2,1)S(1)}, u32[]{:S(2)}, u32[]{:S(2)}) async-start(bf16[8,768,256]{1,2,0:T(8,128)(2,1)} %stack.6), calls=%async_computation.2 | async-start | bytes 6291456 | tf_op jit(solution)/shard_map/all_to_all | solution.py:153
  194.7 1.8 copy.50
  199.2 3.9 %pad_maximum_fusion = bf16[768,2,256]{2,1,0:T(2,128)(2,1)} fusion(bf16[768,1,256]{2,1,0:T(2,128)(2,1)} %copy.50, bf16[768,1,256]{2,1,0:T(2,128)(2,1)} %copy.49), kind=kLoop, calls=%fused_computation.67 | loop fusion | flops 1572864 | bytes 1572864 | tf_op jit(solution)/shard_map/stack | solution.py:102
  203.1 27.8 %all-to-all-done.2 = bf16[8,768,256]{1,2,0:T(8,128)(2,1)S(1)} async-done(((bf16[8,768,256]{1,2,0:T(8,128)(2,1)}), bf16[8,768,256]{1,2,0:T(8,128)(2,1)S(1)}, u32[]{:S(2)}, u32[]{:S(2)}) %all-to-all-start.2) | async-done | bytes 3145760 | tf_op jit(solution)/shard_map/all_to_all | solution.py:153
  230.9 3.0 %convolution_convert_fusion = bf16[768,256]{1,0:T(8,128)(2,1)} fusion(bf16[768,2048]{0,1:T(8,128)(2,1)S(1)} %bitcast.130, bf16[2048,1536]{1,0:T(8,128)(2,1)} %bitcast.128), kind=kOutput, calls=%fused_computation.61 | convolution fusion | flops 805502976 | bytes 4587520 | tf_op jit(solution)/shard_map/dot_general | solution.py:156
  (80 shorter events, 30.1 us)
Async XLA Ops:
  7.2 27.5 %copy-start.6 = (s32[16]{0:T(128)S(1)}, s32[16]{0:T(128)}, u32[]{:S(2)}) copy-start(s32[16]{0:T(128)} %param.21) | copy-start | bytes 196
  7.2 30.2 %copy-start.5 = (f32[2048]{0:T(1024)S(1)}, f32[2048]{0:T(1024)}, u32[]{:S(2)}) copy-start(f32[2048]{0:T(1024)} %param.13) | copy-start | bytes 24580
  7.2 30.2 %copy-start.7 = (s32[1,24]{1,0:T(1,128)S(1)}, s32[1,24]{1,0:T(1,128)}, u32[]{:S(2)}) copy-start(s32[1,24]{1,0:T(1,128)} %param.18) | copy-start | bytes 292
  7.2 101.3 %all-gather.3.cloned.1.call-start = ((), (), s32[]{:S(2)}) async-start(), calls=%async_computation.3 | async-start | bytes 6684672 | tf_op jit(solution)/shard_map/all_gather | solution.py:83
  23.4 48.2 %all-to-all-start = ((bf16[8,768,256]{2,1,0:T(8,128)(2,1)}), bf16[8,768,256]{2,1,0:T(8,128)(2,1)}, u32[]{:S(2)}, u32[]{:S(2)}) async-start(bf16[8,768,256]{2,1,0:T(8,128)(2,1)} %broadcast_in_dim.157), calls=%async_computation | async-start | bytes 6291456 | tf_op jit(solution)/shard_map/all_to_all | solution.py:45
  112.0 3.3 %copy-start = (bf16[4,16,32,1536]{3,2,1,0:T(8,128)(2,1)}, bf16[4,16,32,1536]{3,2,1,0:T(8,128)(2,1)S(1)}, u32[]{:S(2)}) copy-start(bf16[4,16,32,1536]{3,2,1,0:T(8,128)(2,1)S(1)} %copy.42) | copy-start | bytes 18874372
  124.0 1.4 copy-start.2
  124.0 6.1 %copy-start.1 = (pred[768,768]{0,1:T(8,128)(4,1)S(1)}, pred[768,768]{0,1:T(8,128)(4,1)}, u32[]{:S(2)}) copy-start(pred[768,768]{0,1:T(8,128)(4,1)} %iota_compare_fusion) | copy-start | bytes 1769476
  125.5 6.4 %copy-start.3 = (bf16[768,4,48]{0,2,1:T(8,128)(2,1)}, bf16[768,4,48]{0,2,1:T(8,128)(2,1)S(1)}, u32[]{:S(2)}) copy-start(bf16[768,4,48]{0,2,1:T(8,128)(2,1)S(1)} %slice.113) | copy-start | bytes 884740
  130.1 4.2 %copy-start.4 = (bf16[768,4,16]{0,2,1:T(8,128)(2,1)}, bf16[768,4,16]{0,2,1:T(8,128)(2,1)S(1)}, u32[]{:S(2)}) copy-start(bf16[768,4,16]{0,2,1:T(8,128)(2,1)S(1)} %fusion.62) | copy-start | bytes 294916
  185.3 45.6 %all-to-all-start.2 = ((bf16[8,768,256]{1,2,0:T(8,128)(2,1)}), bf16[8,768,256]{1,2,0:T(8,128)(2,1)S(1)}, u32[]{:S(2)}, u32[]{:S(2)}) async-start(bf16[8,768,256]{1,2,0:T(8,128)(2,1)} %stack.6), calls=%async_computation.2 | async-start | bytes 6291456 | tf_op jit(solution)/shard_map/all_to_all | solution.py:153
Sparse Core Ops, SparseCore 0:
  20.7 87.7 all-gather.2
